TPU v7x, 32 devices: a whole 2x2x4 slice. The times are simulated.
32 devices in a mesh: node: 8 (over z, x), feat: 4 (over y, core).
Axes of the slice: x: 2, y: 2, z: 4, core: 2. Of those that a mesh axis runs over, the one named last changes fastest.
Arguments:
- features: bfloat16 [128, 128, 128], P('node', 'feat'), may hold values from -6 to 6
- tile_values: bfloat16 [2048, 128, 128], P('node'), may hold values from -0.125 to 0.125
- tile_row: int32 [2048], P('node'), may hold values from 0 to 127, as said below
- tile_col: int32 [2048], P('node'), may hold values from 0 to 127, as said below
- tile_count: int32 [8], P('node'), may hold values from 32 to 256, as said below
- weight: float32 [128, 128], P('feat'), may hold values from -0.5 to 0.5
- first_moment: float32 [128, 128], P('feat'), may hold values from -3 to 3
- second_moment: float32 [128, 128], P('feat'), may hold values from 0.1 to 2
- cotangent: bfloat16 [128, 128, 128], P('node', 'feat'), may hold values from -6 to 6
Outputs:
- activated: bfloat16 [128, 128, 128], P('node', 'feat')
- feature_grad: float32 [128, 128, 128], P('node', 'feat')
- new_weight: float32 [128, 128], P('feat')
- new_first: float32 [128, 128], P('feat')
- new_second: float32 [128, 128], P('feat')
Inputs may be any that keep to these rules, and one draw needn't show every extreme that they name: `tile_row`: the slots of index d of node (slots d * 256 to (d + 1) * 256 - 1) name target blocks of that index only: d * 16 to (d + 1) * 16 - 1. `tile_col`: A slot's source block lies on an index of node at most 2 away from the slot's own index around the closed loop of node indices; both distances 2 occur on every index. `tile_count`: some index of node has all 256 slots live, some has 32.
All inputs are finite; a program needn't handle non-finite values.
Results may differ from a plain program's by a relative error of at most 0.0058.
Values may be sent and summed in bfloat16 or wider, within the bound.
No kernel may reach another device: no remote copies, remote signals or barrier semaphores. Data moves between devices by JAX's collectives and lax.ppermute only.
A program may use at most 64 MiB of HBM per device.

v0:
```python
import math
import jax
import jax.numpy as jnp
from jax import lax
from jax.sharding import PartitionSpec as P

REACH = 2
first_decay = 0.9
second_decay = 0.999
learn_rate = 0.05
first_fix = 1.0 - 0.9**10
second_fix = 1.0 - 0.999**10
adam_eps = 1e-08


def passed_along(block, axis, distance):
    devices = range(lax.axis_size(axis))
    route = [((i - distance) % len(devices), i) for i in devices]
    return lax.ppermute(block, axis, route)


def elu_slope(preact):
    return jnp.where(preact > 0, 1.0, jnp.exp(jnp.minimum(preact, 0.0)))


def one_hot_table(indices, count, dtype):
    return (indices[:, None] == jnp.arange(count)[None, :]).astype(dtype)


def per_device(
    features,
    tile_values,
    tile_row,
    tile_col,
    tile_count,
    weight,
    first_moment,
    second_moment,
    cotangent,
):
    cycle_size = lax.axis_size("node")
    own_node = lax.axis_index("node")
    blocks = features.shape[0]
    width_local = features.shape[1]
    tile_size = features.shape[2]
    slots = tile_values.shape[0]
    live = (jnp.arange(slots) < tile_count[0]).astype(jnp.float32)
    local_row = tile_row - own_node * blocks
    col_owner = tile_col // blocks
    col_block = tile_col % blocks
    offset = (col_owner - own_node) % cycle_size
    offset = jnp.where(offset > cycle_size // 2, offset - cycle_size, offset)
    source_slot = (offset + REACH) * blocks + col_block
    targets = (2 * REACH + 1) * blocks
    pick_source = one_hot_table(source_slot, targets, jnp.bfloat16)
    pick_row = one_hot_table(local_row, blocks, jnp.bfloat16)
    add_row = one_hot_table(local_row, blocks, jnp.float32) * live[:, None]
    add_source = one_hot_table(source_slot, targets, jnp.float32) * live[:, None]
    pieces = []
    for distance in range(-REACH, REACH + 1):
        if distance == 0:
            pieces.append(features)
        else:
            pieces.append(passed_along(features, "node", -distance))
    nearby = jnp.concatenate(pieces, axis=0)
    sources = jnp.einsum(
        "ts,sfk->tfk", pick_source, nearby, preferred_element_type=jnp.float32
    ).astype(jnp.bfloat16)
    forward_terms = jnp.einsum(
        "tfk,tjk->tfj", sources, tile_values, preferred_element_type=jnp.float32
    )
    aggregate = jnp.einsum("tb,tfj->bfj", add_row, forward_terms, precision=lax.Precision.HIGHEST)
    aggregate = aggregate.astype(jnp.bfloat16)
    weight_half = weight.astype(jnp.bfloat16)
    aggregate_all, weight_all = (
        lax.all_gather(aggregate, "feat", axis=1, tiled=True),
        lax.all_gather(weight_half, "feat", axis=0, tiled=True),
    )
    column_start = lax.axis_index("feat") * width_local
    weight_cols = lax.dynamic_slice_in_dim(weight_all, column_start, width_local, 1)
    preact = jnp.einsum(
        "bij,io->boj", aggregate_all, weight_cols, preferred_element_type=jnp.float32
    )
    activated = jax.nn.elu(preact).astype(jnp.bfloat16)
    slope_grad = (cotangent.astype(jnp.float32) * elu_slope(preact)).astype(jnp.bfloat16)
    slope_all = lax.all_gather(slope_grad, "feat", axis=1, tiled=True)
    node_total = cycle_size * blocks * tile_size
    grad_local = jnp.einsum("bij,boj->io", aggregate, slope_all, preferred_element_type=jnp.float32)
    grad = lax.psum(grad_local, "node") * (1.0 / math.sqrt(node_total))
    back_rows = jnp.einsum(
        "io,boj->bij", weight_half, slope_all, preferred_element_type=jnp.float32
    ).astype(jnp.bfloat16)
    back_sources = jnp.einsum(
        "tb,bfj->tfj", pick_row, back_rows, preferred_element_type=jnp.float32
    ).astype(jnp.bfloat16)
    back_terms = jnp.einsum(
        "tfj,tjk->tfk", back_sources, tile_values, preferred_element_type=jnp.float32
    )
    outgoing = jnp.einsum("ts,tfk->sfk", add_source, back_terms, precision=lax.Precision.HIGHEST)
    outgoing = outgoing.reshape(2 * REACH + 1, blocks, width_local, tile_size)
    feature_grad = outgoing[REACH]
    for distance in range(-REACH, REACH + 1):
        if distance != 0:
            feature_grad = feature_grad + passed_along(outgoing[distance + REACH], "node", distance)
    new_first = first_decay * first_moment + (1.0 - first_decay) * grad
    new_second = second_decay * second_moment + (1.0 - second_decay) * grad * grad
    new_weight = weight - learn_rate * (new_first / first_fix) / (
        jnp.sqrt(new_second / second_fix) + adam_eps
    )
    return (activated, feature_grad, new_weight, new_first, new_second)


def solution(mesh):
    return jax.shard_map(
        per_device,
        mesh=mesh,
        in_specs=(
            P("node", "feat", None),
            P("node", None, None),
            P("node"),
            P("node"),
            P("node"),
            P("feat", None),
            P("feat", None),
            P("feat", None),
            P("node", "feat", None),
        ),
        out_specs=(
            P("node", "feat", None),
            P("node", "feat", None),
            P("feat", None),
            P("feat", None),
            P("feat", None),
        ),
        check_vma=False,
    )
```

profile of v0, /device:TPU:0, one launch (start us, length us, event | category | flops | bytes accessed | tf_op | source)
XLA Modules:
  0.0 112.7 jit_solution(17020929460422994571)
XLA Ops:
  0.6 6.0 %collective-permute-start.2 = (bf16[16,32,128]{2,1,0:T(8,128)(2,1)}, bf16[16,32,128]{2,1,0:T(8,128)(2,1)S(1)}, u32[]{:S(2)}, u32[]{:S(2)}) collective-permute-start(bf16[16,32,128]{2,1,0:T(8,128)(2,1)} %param.9), channel_id=1, source_target_pairs={{4,0},{8,4},{12,8},{16,12},{20,16},{24,20},{28,24},{0,28},{5,1},{9... | collective-permute-start | bytes 393224 | tf_op jit(solution)/shard_map/ppermute | solution.py:19
  6.7 0.0 collective-permute-start.1
  6.7 0.0 collective-permute-start
  6.7 3.8 %collective-permute-start.3 = (bf16[16,32,128]{2,1,0:T(8,128)(2,1)}, bf16[16,32,128]{2,1,0:T(8,128)(2,1)S(1)}, u32[]{:S(2)}, u32[]{:S(2)}) collective-permute-start(bf16[16,32,128]{2,1,0:T(8,128)(2,1)} %param.9), channel_id=1, source_target_pairs={{8,0},{12,4},{16,8},{20,12},{24,16},{28,20},{0,24},{4,28},{9,1},{1... | collective-permute-start | bytes 393224 | tf_op jit(solution)/shard_map/ppermute | solution.py:19
  10.5 0.7 fusion.41
  11.2 0.7 broadcast_subtract_fusion
  12.5 0.7 convert_element_type.38
  13.3 5.2 %all_gather.9 = bf16[128,128]{1,0:T(8,128)(2,1)S(1)} all-gather(bf16[32,128]{1,0:T(8,128)(2,1)S(1)} %convert_element_type.38), channel_id=1, replica_groups=mesh['node'=8,'feat'=4] {'feat'}, dimensions={0}, use_global_device_ids=true | all-gather | bytes 40960 | tf_op jit(solution)/shard_map/all_gather | solution.py:77
  18.4 0.0 collective-permute-done
  18.5 0.0 collective-permute-done.1
  18.5 0.9 constant_dynamic-update-slice_fusion.2
  19.4 0.0 collective-permute-done.2
  19.5 0.0 collective-permute-done.3
  19.5 0.8 fusion.10
  20.3 7.2 %fusion.4 = f32[256,32,128]{2,1,0:T(8,128)S(1)} fusion(bf16[256,128,128]{2,1,0:T(8,128)(2,1)} %param.10, bf16[256,32,128]{2,0,1:T(8,128)(2,1)S(1)} %fusion.10), kind=kOutput, calls=%fused_computation.6 | convolution fusion | flops 268435456 | bytes 14680064 | tf_op jit(solution)/shard_map/tfk,tjk->tfj/dot_general | solution.py:69
  27.5 0.0 copy-start.1
  27.5 4.4 %fusion.7 = bf16[16,32,128]{2,0,1:T(8,128)(2,1)S(1)} fusion(f32[256,32,128]{2,1,0:T(8,128)S(1)} %fusion.4, f32[256]{0:T(256)S(1)} %compare_convert_fusion, s32[256]{0:T(256)S(1)} %broadcast_subtract_fusion), kind=kOutput, calls=%fused_computation.11 | convolution fusion | flops 201400320 | bytes 4327424 | tf_op jit(solution)/shard_map/tb,tfj->bfj/dot_general | solution.py:72
  31.9 7.3 %all_gather.10 = bf16[16,128,128]{2,0,1:T(8,128)(2,1)S(1)} all-gather(bf16[16,32,128]{2,0,1:T(8,128)(2,1)S(1)} %fusion.7), channel_id=1, replica_groups=mesh['node'=8,'feat'=4] {'feat'}, dimensions={1}, use_global_device_ids=true | all-gather | bytes 655360 | tf_op jit(solution)/shard_map/all_gather | solution.py:76
  39.1 0.0 copy-done.1
  39.1 1.1 fusion.16
  40.2 7.5 %all_gather.11 = bf16[16,128,128]{2,1,0:T(8,128)(2,1)S(1)} all-gather(bf16[16,32,128]{2,1,0:T(8,128)(2,1)S(1)} %get-tuple-element.22), channel_id=1, replica_groups=mesh['node'=8,'feat'=4] {'feat'}, dimensions={1}, use_global_device_ids=true | all-gather | bytes 655360 | tf_op jit(solution)/shard_map/all_gather | solution.py:86
  47.7 0.3 fusion.6
  48.0 0.2 copy.25
  48.3 0.7 fusion.34
  49.0 7.2 %fusion.5 = f32[256,32,128]{2,1,0:T(8,128)S(1)} fusion(bf16[256,128,128]{2,1,0:T(8,128)(2,1)} %param.10, bf16[256,32,128]{2,0,1:T(8,128)(2,1)S(1)} %fusion.34), kind=kOutput, calls=%fused_computation.7 | convolution fusion | flops 268435456 | bytes 14680064 | tf_op jit(solution)/shard_map/tfj,tjk->tfk/dot_general | solution.py:96
  56.2 0.0 copy-start
  56.2 4.9 %fusion = f32[80,32,128]{2,0,1:T(8,128)S(1)} fusion(f32[256,32,128]{2,1,0:T(8,128)S(1)} %fusion.5, f32[256]{0:T(256)S(1)} %compare_convert_fusion, s32[256]{0:T(256)S(1)} %fusion.41), kind=kOutput, calls=%fused_computation | convolution fusion | flops 1006673920 | bytes 5507072 | tf_op jit(solution)/shard_map/ts,tfk->sfk/dot_general | solution.py:99
  61.1 0.9 fusion.48
  62.0 0.0 collective-permute-start.4
  62.0 2.0 %collective-permute-start.7 = (f32[16,32,128]{2,0,1:T(8,128)}, f32[16,32,128]{2,0,1:T(8,128)S(1)}, u32[]{:S(2)}, u32[]{:S(2)}) collective-permute-start(f32[16,32,128]{2,0,1:T(8,128)} %get-tuple-element.19), channel_id=1, source_target_pairs={{24,0},{28,4},{0,8},{4,12},{8,16},{12,20},{16,24},{20,28},{25,1},{... | collective-permute-start | bytes 786440 | tf_op jit(solution)/shard_map/ppermute | solution.py:19
  64.0 1.5 %collective-permute-start.6 = (f32[16,32,128]{2,0,1:T(8,128)S(1)}, f32[16,32,128]{2,0,1:T(8,128)S(1)}, u32[]{:S(2)}, u32[]{:S(2)}) collective-permute-start(f32[16,32,128]{2,0,1:T(8,128)S(1)} %get-tuple-element.20), channel_id=1, source_target_pairs={{28,0},{0,4},{4,8},{8,12},{12,16},{16,20},{20,24},{24,28},{29,1},{... | collective-permute-start | bytes 786440 | tf_op jit(solution)/shard_map/ppermute | solution.py:19
  65.5 3.3 %collective-permute-start.5 = (f32[16,32,128]{2,0,1:T(8,128)S(1)}, f32[16,32,128]{2,0,1:T(8,128)S(1)}, u32[]{:S(2)}, u32[]{:S(2)}) collective-permute-start(f32[16,32,128]{2,0,1:T(8,128)S(1)} %get-tuple-element.21), channel_id=1, source_target_pairs={{4,0},{8,4},{12,8},{16,12},{20,16},{24,20},{28,24},{0,28},{5,1},{9... | collective-permute-start | bytes 786440 | tf_op jit(solution)/shard_map/ppermute | solution.py:19
  68.8 0.9 convolution_bitcast_fusion.1
  69.7 40.8 %psum.7 = f32[32,128]{1,0:T(8,128)S(1)} all-reduce(f32[32,128]{1,0:T(8,128)} %convolution_bitcast_fusion.1), channel_id=1, replica_groups=mesh['node'=8,'feat'=4] {'node'}, use_global_device_ids=true, to_apply=%region_0.1 | all-reduce | flops 4096 | bytes 32768 | tf_op jit(solution)/shard_map/psum | solution.py:89
  110.4 0.0 copy-done
  110.4 1.4 %divide_subtract_fusion = (f32[32,128]{1,0:T(8,128)}, f32[32,128]{1,0:T(8,128)}, f32[32,128]{1,0:T(8,128)}) fusion(f32[32,128]{1,0:T(8,128)S(1)} %copy-done, f32[32,128]{1,0:T(8,128)S(1)} %psum.7, f32[32,128]{1,0:T(8,128)} %param.15, f32[32,128]{1,0:T(8,128)} %param.16), kind=kLoop, calls=%fused_computation.39 | loop fusion | flops 53248 | bytes 114688 | tf_op jit(solution)/shard_map/sub | solution.py:107
  111.8 0.0 collective-permute-done.4
  111.8 0.0 collective-permute-done.7
  111.8 0.0 collective-permute-done.6
  111.8 0.0 collective-permute-done.5
  111.8 0.1 fusion.19
  111.9 0.8 copy.21
  (5 shorter events, 0.1 us)
Async XLA Ops:
  0.6 18.8 %collective-permute-start.2 = (bf16[16,32,128]{2,1,0:T(8,128)(2,1)}, bf16[16,32,128]{2,1,0:T(8,128)(2,1)S(1)}, u32[]{:S(2)}, u32[]{:S(2)}) collective-permute-start(bf16[16,32,128]{2,1,0:T(8,128)(2,1)} %param.9), channel_id=1, source_target_pairs={{4,0},{8,4},{12,8},{16,12},{20,16},{24,20},{28,24},{0,28},{5,1},{9... | collective-permute-start | bytes 393224 | tf_op jit(solution)/shard_map/ppermute | solution.py:19
  6.7 11.8 %collective-permute-start.1 = (bf16[16,32,128]{2,1,0:T(8,128)(2,1)}, bf16[16,32,128]{2,1,0:T(8,128)(2,1)S(1)}, u32[]{:S(2)}, u32[]{:S(2)}) collective-permute-start(bf16[16,32,128]{2,1,0:T(8,128)(2,1)} %param.9), channel_id=1, source_target_pairs={{28,0},{0,4},{4,8},{8,12},{12,16},{16,20},{20,24},{24,28},{29,1},{... | collective-permute-start | bytes 393224 | tf_op jit(solution)/shard_map/ppermute | solution.py:19
  6.7 11.8 %collective-permute-start = (bf16[16,32,128]{2,1,0:T(8,128)(2,1)}, bf16[16,32,128]{2,1,0:T(8,128)(2,1)S(1)}, u32[]{:S(2)}, u32[]{:S(2)}) collective-permute-start(bf16[16,32,128]{2,1,0:T(8,128)(2,1)} %param.9), channel_id=1, source_target_pairs={{24,0},{28,4},{0,8},{4,12},{8,16},{12,20},{16,24},{20,28},{25,1},{... | collective-permute-start | bytes 393224 | tf_op jit(solution)/shard_map/ppermute | solution.py:19
  6.7 12.8 %collective-permute-start.3 = (bf16[16,32,128]{2,1,0:T(8,128)(2,1)}, bf16[16,32,128]{2,1,0:T(8,128)(2,1)S(1)}, u32[]{:S(2)}, u32[]{:S(2)}) collective-permute-start(bf16[16,32,128]{2,1,0:T(8,128)(2,1)} %param.9), channel_id=1, source_target_pairs={{8,0},{12,4},{16,8},{20,12},{24,16},{28,20},{0,24},{4,28},{9,1},{1... | collective-permute-start | bytes 393224 | tf_op jit(solution)/shard_map/ppermute | solution.py:19
  27.5 11.6 %copy-start.1 = (bf16[16,32,128]{2,1,0:T(8,128)(2,1)S(1)}, bf16[16,32,128]{2,1,0:T(8,128)(2,1)}, u32[]{:S(2)}) copy-start(bf16[16,32,128]{2,1,0:T(8,128)(2,1)} %param.17) | copy-start | bytes 393220
  56.2 54.2 %copy-start = (f32[32,128]{1,0:T(8,128)S(1)}, f32[32,128]{1,0:T(8,128)}, u32[]{:S(2)}) copy-start(f32[32,128]{1,0:T(8,128)} %param.14) | copy-start | bytes 49156
  62.0 49.8 %collective-permute-start.4 = (f32[16,32,128]{2,0,1:T(8,128)}, f32[16,32,128]{2,0,1:T(8,128)S(1)}, u32[]{:S(2)}, u32[]{:S(2)}) collective-permute-start(f32[16,32,128]{2,0,1:T(8,128)} %get-tuple-element.18), channel_id=1, source_target_pairs={{8,0},{12,4},{16,8},{20,12},{24,16},{28,20},{0,24},{4,28},{9,1},{1... | collective-permute-start | bytes 786440 | tf_op jit(solution)/shard_map/ppermute | solution.py:19
  62.0 49.8 %collective-permute-start.7 = (f32[16,32,128]{2,0,1:T(8,128)}, f32[16,32,128]{2,0,1:T(8,128)S(1)}, u32[]{:S(2)}, u32[]{:S(2)}) collective-permute-start(f32[16,32,128]{2,0,1:T(8,128)} %get-tuple-element.19), channel_id=1, source_target_pairs={{24,0},{28,4},{0,8},{4,12},{8,16},{12,20},{16,24},{20,28},{25,1},{... | collective-permute-start | bytes 786440 | tf_op jit(solution)/shard_map/ppermute | solution.py:19
  64.0 47.7 %collective-permute-start.6 = (f32[16,32,128]{2,0,1:T(8,128)S(1)}, f32[16,32,128]{2,0,1:T(8,128)S(1)}, u32[]{:S(2)}, u32[]{:S(2)}) collective-permute-start(f32[16,32,128]{2,0,1:T(8,128)S(1)} %get-tuple-element.20), channel_id=1, source_target_pairs={{28,0},{0,4},{4,8},{8,12},{12,16},{16,20},{20,24},{24,28},{29,1},{... | collective-permute-start | bytes 786440 | tf_op jit(solution)/shard_map/ppermute | solution.py:19
  65.5 46.3 %collective-permute-start.5 = (f32[16,32,128]{2,0,1:T(8,128)S(1)}, f32[16,32,128]{2,0,1:T(8,128)S(1)}, u32[]{:S(2)}, u32[]{:S(2)}) collective-permute-start(f32[16,32,128]{2,0,1:T(8,128)S(1)} %get-tuple-element.21), channel_id=1, source_target_pairs={{4,0},{8,4},{12,8},{16,12},{20,16},{24,20},{28,24},{0,28},{5,1},{9... | collective-permute-start | bytes 786440 | tf_op jit(solution)/shard_map/ppermute | solution.py:19
where the time goes:
time: 113 us
  blocking collectives  60.6 us (54%)
  matrix products  27.5 us (24%)
  starting transfers between devices  16.6 us (15%)
  other arithmetic  3.56 us (3%)
  local copies, waits for them, and re-layouts  2.92 us (3%)
  between operations  1.42 us (1%)
    psum x1, blocking collectives, per_device(): grad = lax.psum(grad_local, 'node') * (1.0 / math.sqrt(node_total))  40.8 us
    ppermute x8, starting transfers between devices, passed_along(): return lax.ppermute(block, axis, route)  16.6 us
    all_gather x1, blocking collectives, per_device(): slope_all = lax.all_gather(slope_grad, 'feat', axis=1, tiled=True)  7.46 us
    all_gather x1, blocking collectives, per_device(): lax.all_gather(aggregate, 'feat', axis=1, tiled=True)  7.25 us
    dot_general x1, matrix products, per_device(): jnp.einsum('tfk,tjk->tfj', sources, tile_values, preferred_element_type=j...  7.25 us
    dot_general x1, matrix products, per_device(): jnp.einsum('tfj,tjk->tfk', back_sources, tile_values, preferred_element_t...  7.21 us
    all_gather x1, blocking collectives, per_device(): lax.all_gather(weight_half, 'feat', axis=0, tiled=True)  5.18 us
    dot_general x1, matrix products, per_device(): jnp.einsum('ts,tfk->sfk', add_source, back_terms, precision=lax.Precision...  4.89 us
  transfers between devices with their start and end apart: 8, of which 0 were waited for; matrix products, arithmetic and copies ran while one was open for 5% of the time, Pallas kernels for 0%

commit v1 on v0

--- a/solution.py
+++ b/solution.py
@@ -11,6 +11,28 @@
 first_fix = 1.0 - 0.9**10
 second_fix = 1.0 - 0.999**10
 adam_eps = 1e-08
+
+
+def laid_out(pieces, dim):
+    pieces = jnp.moveaxis(pieces, 0, dim)
+    dims = pieces.shape
+    return pieces.reshape(*dims[:dim], dims[dim] * dims[dim + 1], *dims[dim + 2 :])
+
+
+def ring_gather(shard, axis, dim):
+    size = lax.axis_size(axis)
+    pairs = [(i, (i + 1) % size) for i in range(size)]
+    back = [(b, a) for a, b in pairs]
+    lower, upper = ([], [])
+    for step in range(size - 1):
+        if step % 2 == 0:
+            lower.append(lax.ppermute(lower[-1] if lower else shard, axis, pairs))
+        else:
+            upper.append(lax.ppermute(upper[-1] if upper else shard, axis, back))
+    parts = jnp.stack([*lower[::-1], shard, *upper])
+    shift = lax.axis_index(axis) - len(lower)
+    parts = parts[(jnp.arange(size) - shift) % size]
+    return laid_out(parts, dim)
 
 
 def passed_along(block, axis, distance):
@@ -73,7 +95,7 @@
     aggregate = aggregate.astype(jnp.bfloat16)
     weight_half = weight.astype(jnp.bfloat16)
     aggregate_all, weight_all = (
-        lax.all_gather(aggregate, "feat", axis=1, tiled=True),
+        ring_gather(aggregate, "feat", 1),
         lax.all_gather(weight_half, "feat", axis=0, tiled=True),
     )
     column_start = lax.axis_index("feat") * width_local

time: 113 us -> 117 us (1.035)
  waiting for transfers between devices: 0.02 us -> 6.21 us
  blocking collectives: 60.6 us -> 55.9 us
  starting transfers between devices: 16.6 us -> 18.8 us
    all_gather x1 -> x0, blocking collectives: 7.25 us -> none  [per_device(): lax.all_gather(aggregate, 'feat', axis=1, tiled=True)]
    ppermute x8, waiting for transfers between devices: 0.02 us -> 3.56 us  [passed_along(): return lax.ppermute(block, axis, route)]
    ppermute x0 -> x3, waiting for transfers between devices: none -> 2.65 us  [the longest x2 2.65 us: ring_gather(): lower.append(lax.ppermute(lower[-1] if lower else shard, axis, pairs))]
    ppermute x0 -> x3, starting transfers between devices: none -> 1.77 us  [the longest x1 1.73 us: ring_gather(): upper.append(lax.ppermute(upper[-1] if upper else shard, axis, back))]
    psum x1, blocking collectives: 40.8 us -> 42.5 us  [per_device(): grad = lax.psum(grad_local, 'node') * (1.0 / math.sqrt(node_total))]
  transfers between devices with their start and end apart: 8 -> 11, of which waited for: 0 -> 3; matrix products, arithmetic and copies ran while one was open for 5% -> 4% of each run, Pallas kernels for 0% -> 0%
where the time goes in v1:
time: 117 us; the launch traced here: 116 us
  blocking collectives  55.9 us (48%)
  matrix products  27.5 us (24%)
  starting transfers between devices  18.8 us (16%)
  waiting for transfers between devices  6.21 us (5%)
  local copies, waits for them, and re-layouts  3.55 us (3%)
  other arithmetic  2.93 us (3%)
  between operations  1.48 us (1%)
    psum x1, blocking collectives, per_device(): grad = lax.psum(grad_local, 'node') * (1.0 / math.sqrt(node_total))  42.5 us
    ppermute x8, starting transfers between devices, passed_along(): return lax.ppermute(block, axis, route)  17 us
    all_gather x1, blocking collectives, per_device(): slope_all = lax.all_gather(slope_grad, 'feat', axis=1, tiled=True)  7.3 us
    dot_general x1, matrix products, per_device(): jnp.einsum('tfk,tjk->tfj', sources, tile_values, preferred_element_type=j...  7.25 us
    dot_general x1, matrix products, per_device(): jnp.einsum('tfj,tjk->tfk', back_sources, tile_values, preferred_element_t...  7.21 us
    all_gather x1, blocking collectives, per_device(): lax.all_gather(weight_half, 'feat', axis=0, tiled=True)  6.11 us
    dot_general x1, matrix products, per_device(): jnp.einsum('ts,tfk->sfk', add_source, back_terms, precision=lax.Precision...  4.89 us
    dot_general x1, matrix products, per_device(): jnp.einsum('tb,tfj->bfj', add_row, forward_terms, precision=lax.Precision...  4.35 us
  transfers between devices with their start and end apart: 11, of which 3 were waited for; matrix products, arithmetic and copies ran while one was open for 4% of the time, Pallas kernels for 0%

profile of v1, /device:TPU:0, one launch (start us, length us, event | category | flops | bytes accessed | tf_op | source)
XLA Modules:
  0.0 116.4 jit_solution(426708267641238286)
XLA Ops:
  0.6 6.0 %collective-permute-start.2 = (bf16[16,32,128]{2,1,0:T(8,128)(2,1)}, bf16[16,32,128]{2,1,0:T(8,128)(2,1)S(1)}, u32[]{:S(2)}, u32[]{:S(2)}) collective-permute-start(bf16[16,32,128]{2,1,0:T(8,128)(2,1)} %param.9), channel_id=1, source_target_pairs={{4,0},{8,4},{12,8},{16,12},{20,16},{24,20},{28,24},{0,28},{5,1},{9... | collective-permute-start | bytes 393224 | tf_op jit(solution)/shard_map/ppermute | solution.py:41
  6.7 0.0 collective-permute-start.1
  6.7 0.0 collective-permute-start
  6.7 3.8 %collective-permute-start.3 = (bf16[16,32,128]{2,1,0:T(8,128)(2,1)}, bf16[16,32,128]{2,1,0:T(8,128)(2,1)S(1)}, u32[]{:S(2)}, u32[]{:S(2)}) collective-permute-start(bf16[16,32,128]{2,1,0:T(8,128)(2,1)} %param.9), channel_id=1, source_target_pairs={{8,0},{12,4},{16,8},{20,12},{24,16},{28,20},{0,24},{4,28},{9,1},{1... | collective-permute-start | bytes 393224 | tf_op jit(solution)/shard_map/ppermute | solution.py:41
  10.5 0.7 fusion.41
  11.2 0.7 broadcast_subtract_fusion
  12.5 2.5 %collective-permute-done = bf16[16,32,128]{2,1,0:T(8,128)(2,1)S(1)} collective-permute-done((bf16[16,32,128]{2,1,0:T(8,128)(2,1)}, bf16[16,32,128]{2,1,0:T(8,128)(2,1)S(1)}, u32[]{:S(2)}, u32[]{:S(2)}) %collective-permute-start) | collective-permute-done | bytes 131104 | tf_op jit(solution)/shard_map/ppermute | solution.py:41
  15.1 1.0 collective-permute-done.1
  16.1 0.9 constant_dynamic-update-slice_fusion.2
  17.0 0.0 collective-permute-done.2
  17.1 0.0 collective-permute-done.3
  17.1 0.8 fusion.10
  17.9 7.2 %fusion.4 = f32[256,32,128]{2,1,0:T(8,128)S(1)} fusion(bf16[256,128,128]{2,1,0:T(8,128)(2,1)} %param.10, bf16[256,32,128]{2,0,1:T(8,128)(2,1)S(1)} %fusion.10), kind=kOutput, calls=%fused_computation.7 | convolution fusion | flops 268435456 | bytes 14680064 | tf_op jit(solution)/shard_map/tfk,tjk->tfj/dot_general | solution.py:91
  25.1 0.0 copy-start
  25.2 0.0 copy-start.1
  25.2 4.4 %fusion.7 = bf16[16,32,128]{2,0,1:T(8,128)(2,1)S(1)} fusion(f32[256,32,128]{2,1,0:T(8,128)S(1)} %fusion.4, f32[256]{0:T(256)S(1)} %compare_convert_fusion, s32[256]{0:T(256)S(1)} %broadcast_subtract_fusion), kind=kOutput, calls=%fused_computation.12 | convolution fusion | flops 201400320 | bytes 4327424 | tf_op jit(solution)/shard_map/tb,tfj->bfj/dot_general | solution.py:94
  29.5 0.0 collective-permute-start.4
  29.6 1.7 %collective-permute-start.6 = (bf16[16,32,128]{2,0,1:T(8,128)(2,1)S(1)}, bf16[16,32,128]{2,0,1:T(8,128)(2,1)S(1)}, u32[]{:S(2)}, u32[]{:S(2)}) collective-permute-start(bf16[16,32,128]{2,0,1:T(8,128)(2,1)S(1)} %fusion.7), channel_id=1, source_target_pairs={{1,0},{2,1},{3,2},{0,3},{5,4},{6,5},{7,6},{4,7},{9,8},{10,9},{11,1... | collective-permute-start | bytes 393224 | tf_op jit(solution)/shard_map/ppermute | solution.py:31
  31.3 2.6 %collective-permute-done.4 = bf16[16,32,128]{2,0,1:T(8,128)(2,1)S(1)} collective-permute-done((bf16[16,32,128]{2,0,1:T(8,128)(2,1)S(1)}, bf16[16,32,128]{2,0,1:T(8,128)(2,1)S(1)}, u32[]{:S(2)}, u32[]{:S(2)}) %collective-permute-start.4) | collective-permute-done | bytes 131104 | tf_op jit(solution)/shard_map/ppermute | solution.py:29
  33.9 0.0 collective-permute-start.5
  34.0 0.0 copy-done
  34.0 6.1 %all_gather.6 = bf16[128,128]{1,0:T(8,128)(2,1)S(1)} all-gather(bf16[32,128]{1,0:T(8,128)(2,1)S(1)} %convert_element_type.38), channel_id=1, replica_groups=mesh['node'=8,'feat'=4] {'feat'}, dimensions={0}, use_global_device_ids=true | all-gather | bytes 40960 | tf_op jit(solution)/shard_map/all_gather | solution.py:99
  40.1 0.0 collective-permute-done.6
  40.1 0.0 collective-permute-done.5
  40.1 0.1 pad_maximum_fusion
  40.2 0.6 gather_fusion
  40.9 0.0 copy-done.1
  40.9 1.1 fusion.16
  42.0 7.3 %all_gather.7 = bf16[16,128,128]{2,1,0:T(8,128)(2,1)S(1)} all-gather(bf16[16,32,128]{2,1,0:T(8,128)(2,1)S(1)} %get-tuple-element.22), channel_id=1, replica_groups=mesh['node'=8,'feat'=4] {'feat'}, dimensions={1}, use_global_device_ids=true | all-gather | bytes 655360 | tf_op jit(solution)/shard_map/all_gather | solution.py:108
  49.3 0.3 fusion.6
  49.6 0.2 copy.25
  49.8 0.7 fusion.34
  50.6 7.2 %fusion.5 = f32[256,32,128]{2,1,0:T(8,128)S(1)} fusion(bf16[256,128,128]{2,1,0:T(8,128)(2,1)} %param.10, bf16[256,32,128]{2,0,1:T(8,128)(2,1)S(1)} %fusion.34), kind=kOutput, calls=%fused_computation.8 | convolution fusion | flops 268435456 | bytes 14680064 | tf_op jit(solution)/shard_map/tfj,tjk->tfk/dot_general | solution.py:118
  57.8 4.9 %fusion = f32[80,32,128]{2,0,1:T(8,128)S(1)} fusion(f32[256,32,128]{2,1,0:T(8,128)S(1)} %fusion.5, f32[256]{0:T(256)S(1)} %compare_convert_fusion, s32[256]{0:T(256)S(1)} %fusion.41), kind=kOutput, calls=%fused_computation.1 | convolution fusion | flops 1006673920 | bytes 5507072 | tf_op jit(solution)/shard_map/ts,tfk->sfk/dot_general | solution.py:121
  62.7 0.9 fusion.50
  63.6 2.5 %collective-permute-start.7 = (f32[16,32,128]{2,0,1:T(8,128)}, f32[16,32,128]{2,0,1:T(8,128)S(1)}, u32[]{:S(2)}, u32[]{:S(2)}) collective-permute-start(f32[16,32,128]{2,0,1:T(8,128)} %get-tuple-element.18), channel_id=1, source_target_pairs={{8,0},{12,4},{16,8},{20,12},{24,16},{28,20},{0,24},{4,28},{9,1},{1... | collective-permute-start | bytes 786440 | tf_op jit(solution)/shard_map/ppermute | solution.py:41
  66.0 0.0 collective-permute-start.10
  66.0 2.9 %collective-permute-start.9 = (f32[16,32,128]{2,0,1:T(8,128)S(1)}, f32[16,32,128]{2,0,1:T(8,128)S(1)}, u32[]{:S(2)}, u32[]{:S(2)}) collective-permute-start(f32[16,32,128]{2,0,1:T(8,128)S(1)} %get-tuple-element.20), channel_id=1, source_target_pairs={{28,0},{0,4},{4,8},{8,12},{12,16},{16,20},{20,24},{24,28},{29,1},{... | collective-permute-start | bytes 786440 | tf_op jit(solution)/shard_map/ppermute | solution.py:41
  68.9 1.9 %collective-permute-start.8 = (f32[16,32,128]{2,0,1:T(8,128)S(1)}, f32[16,32,128]{2,0,1:T(8,128)S(1)}, u32[]{:S(2)}, u32[]{:S(2)}) collective-permute-start(f32[16,32,128]{2,0,1:T(8,128)S(1)} %get-tuple-element.21), channel_id=1, source_target_pairs={{4,0},{8,4},{12,8},{16,12},{20,16},{24,20},{28,24},{0,28},{5,1},{9... | collective-permute-start | bytes 786440 | tf_op jit(solution)/shard_map/ppermute | solution.py:41
  70.7 0.9 convolution_bitcast_fusion.1
  71.6 42.5 %psum.7 = f32[32,128]{1,0:T(8,128)S(1)} all-reduce(f32[32,128]{1,0:T(8,128)} %convolution_bitcast_fusion.1), channel_id=1, replica_groups=mesh['node'=8,'feat'=4] {'node'}, use_global_device_ids=true, to_apply=%region_0.1 | all-reduce | flops 4096 | bytes 32768 | tf_op jit(solution)/shard_map/psum | solution.py:111
  114.1 1.4 %divide_subtract_fusion = (f32[32,128]{1,0:T(8,128)}, f32[32,128]{1,0:T(8,128)}, f32[32,128]{1,0:T(8,128)}) fusion(f32[32,128]{1,0:T(8,128)S(1)} %copy-done, f32[32,128]{1,0:T(8,128)S(1)} %psum.7, f32[32,128]{1,0:T(8,128)} %param.15, f32[32,128]{1,0:T(8,128)} %param.16), kind=kLoop, calls=%fused_computation.41 | loop fusion | flops 53248 | bytes 114688 | tf_op jit(solution)/shard_map/sub | solution.py:129
  115.5 0.0 collective-permute-done.7
  115.5 0.0 collective-permute-done.10
  115.5 0.0 collective-permute-done.9
  115.5 0.0 collective-permute-done.8
  115.5 0.1 fusion.19
  115.6 0.8 copy.21
  (8 shorter events, 0.1 us)
Async XLA Ops:
  0.6 16.4 %collective-permute-start.2 = (bf16[16,32,128]{2,1,0:T(8,128)(2,1)}, bf16[16,32,128]{2,1,0:T(8,128)(2,1)S(1)}, u32[]{:S(2)}, u32[]{:S(2)}) collective-permute-start(bf16[16,32,128]{2,1,0:T(8,128)(2,1)} %param.9), channel_id=1, source_target_pairs={{4,0},{8,4},{12,8},{16,12},{20,16},{24,20},{28,24},{0,28},{5,1},{9... | collective-permute-start | bytes 393224 | tf_op jit(solution)/shard_map/ppermute | solution.py:41
  6.7 9.4 %collective-permute-start.1 = (bf16[16,32,128]{2,1,0:T(8,128)(2,1)}, bf16[16,32,128]{2,1,0:T(8,128)(2,1)S(1)}, u32[]{:S(2)}, u32[]{:S(2)}) collective-permute-start(bf16[16,32,128]{2,1,0:T(8,128)(2,1)} %param.9), channel_id=1, source_target_pairs={{28,0},{0,4},{4,8},{8,12},{12,16},{16,20},{20,24},{24,28},{29,1},{... | collective-permute-start | bytes 393224 | tf_op jit(solution)/shard_map/ppermute | solution.py:41
  6.7 8.4 %collective-permute-start = (bf16[16,32,128]{2,1,0:T(8,128)(2,1)}, bf16[16,32,128]{2,1,0:T(8,128)(2,1)S(1)}, u32[]{:S(2)}, u32[]{:S(2)}) collective-permute-start(bf16[16,32,128]{2,1,0:T(8,128)(2,1)} %param.9), channel_id=1, source_target_pairs={{24,0},{28,4},{0,8},{4,12},{8,16},{12,20},{16,24},{20,28},{25,1},{... | collective-permute-start | bytes 393224 | tf_op jit(solution)/shard_map/ppermute | solution.py:41
  6.7 10.4 %collective-permute-start.3 = (bf16[16,32,128]{2,1,0:T(8,128)(2,1)}, bf16[16,32,128]{2,1,0:T(8,128)(2,1)S(1)}, u32[]{:S(2)}, u32[]{:S(2)}) collective-permute-start(bf16[16,32,128]{2,1,0:T(8,128)(2,1)} %param.9), channel_id=1, source_target_pairs={{8,0},{12,4},{16,8},{20,12},{24,16},{28,20},{0,24},{4,28},{9,1},{1... | collective-permute-start | bytes 393224 | tf_op jit(solution)/shard_map/ppermute | solution.py:41
  25.1 8.8 %copy-start = (f32[32,128]{1,0:T(8,128)S(1)}, f32[32,128]{1,0:T(8,128)}, u32[]{:S(2)}) copy-start(f32[32,128]{1,0:T(8,128)} %param.14) | copy-start | bytes 49156
  25.2 15.7 %copy-start.1 = (bf16[16,32,128]{2,1,0:T(8,128)(2,1)S(1)}, bf16[16,32,128]{2,1,0:T(8,128)(2,1)}, u32[]{:S(2)}) copy-start(bf16[16,32,128]{2,1,0:T(8,128)(2,1)} %param.17) | copy-start | bytes 393220
  29.5 4.4 %collective-permute-start.4 = (bf16[16,32,128]{2,0,1:T(8,128)(2,1)S(1)}, bf16[16,32,128]{2,0,1:T(8,128)(2,1)S(1)}, u32[]{:S(2)}, u32[]{:S(2)}) collective-permute-start(bf16[16,32,128]{2,0,1:T(8,128)(2,1)S(1)} %fusion.7), channel_id=1, source_target_pairs={{0,1},{1,2},{2,3},{3,0},{4,5},{5,6},{6,7},{7,4},{8,9},{9,10},{10,1... | collective-permute-start | bytes 393224 | tf_op jit(solution)/shard_map/ppermute | solution.py:29
  29.6 10.5 %collective-permute-start.6 = (bf16[16,32,128]{2,0,1:T(8,128)(2,1)S(1)}, bf16[16,32,128]{2,0,1:T(8,128)(2,1)S(1)}, u32[]{:S(2)}, u32[]{:S(2)}) collective-permute-start(bf16[16,32,128]{2,0,1:T(8,128)(2,1)S(1)} %fusion.7), channel_id=1, source_target_pairs={{1,0},{2,1},{3,2},{0,3},{5,4},{6,5},{7,6},{4,7},{9,8},{10,9},{11,1... | collective-permute-start | bytes 393224 | tf_op jit(solution)/shard_map/ppermute | solution.py:31
  33.9 6.2 %collective-permute-start.5 = (bf16[16,32,128]{2,0,1:T(8,128)(2,1)S(1)}, bf16[16,32,128]{2,0,1:T(8,128)(2,1)S(1)}, u32[]{:S(2)}, u32[]{:S(2)}) collective-permute-start(bf16[16,32,128]{2,0,1:T(8,128)(2,1)S(1)} %collective-permute-done.4), channel_id=1, source_target_pairs={{0,1},{1,2},{2,3},{3,0},{4,5},{5,6},{6,7},{7,4},{8,9},{9,10},{10,1... | collective-permute-start | bytes 393224 | tf_op jit(solution)/shard_map/ppermute | solution.py:29
  63.6 51.9 %collective-permute-start.7 = (f32[16,32,128]{2,0,1:T(8,128)}, f32[16,32,128]{2,0,1:T(8,128)S(1)}, u32[]{:S(2)}, u32[]{:S(2)}) collective-permute-start(f32[16,32,128]{2,0,1:T(8,128)} %get-tuple-element.18), channel_id=1, source_target_pairs={{8,0},{12,4},{16,8},{20,12},{24,16},{28,20},{0,24},{4,28},{9,1},{1... | collective-permute-start | bytes 786440 | tf_op jit(solution)/shard_map/ppermute | solution.py:41
  66.0 49.5 %collective-permute-start.10 = (f32[16,32,128]{2,0,1:T(8,128)}, f32[16,32,128]{2,0,1:T(8,128)S(1)}, u32[]{:S(2)}, u32[]{:S(2)}) collective-permute-start(f32[16,32,128]{2,0,1:T(8,128)} %get-tuple-element.19), channel_id=1, source_target_pairs={{24,0},{28,4},{0,8},{4,12},{8,16},{12,20},{16,24},{20,28},{25,1},{... | collective-permute-start | bytes 786440 | tf_op jit(solution)/shard_map/ppermute | solution.py:41
  66.0 49.5 %collective-permute-start.9 = (f32[16,32,128]{2,0,1:T(8,128)S(1)}, f32[16,32,128]{2,0,1:T(8,128)S(1)}, u32[]{:S(2)}, u32[]{:S(2)}) collective-permute-start(f32[16,32,128]{2,0,1:T(8,128)S(1)} %get-tuple-element.20), channel_id=1, source_target_pairs={{28,0},{0,4},{4,8},{8,12},{12,16},{16,20},{20,24},{24,28},{29,1},{... | collective-permute-start | bytes 786440 | tf_op jit(solution)/shard_map/ppermute | solution.py:41
  68.9 46.6 %collective-permute-start.8 = (f32[16,32,128]{2,0,1:T(8,128)S(1)}, f32[16,32,128]{2,0,1:T(8,128)S(1)}, u32[]{:S(2)}, u32[]{:S(2)}) collective-permute-start(f32[16,32,128]{2,0,1:T(8,128)S(1)} %get-tuple-element.21), channel_id=1, source_target_pairs={{4,0},{8,4},{12,8},{16,12},{20,16},{24,20},{28,24},{0,28},{5,1},{9... | collective-permute-start | bytes 786440 | tf_op jit(solution)/shard_map/ppermute | solution.py:41
